TPU v7x, 32 devices: a whole 2x2x4 slice. The times are simulated.
32 devices in a mesh: rec: 2 (over y), gx: 16 (over z, x, core).
Axes of the slice: x: 2, y: 2, z: 4, core: 2. Of those that a mesh axis runs over, the one named last changes fastest.
Arguments:
- velocity: float32 [4, 3, 96, 16, 128], P(None, None, ('rec', 'gx')), parts along dimension 2, may hold values from -6 to 36, as said below
- span_rim: float32 [4, 2, 96, 10, 6], P(None, None, ('rec', 'gx')), parts along dimension 2, may hold values from -6 to 36, as said below
- sketch_old: bfloat16 [3, 96, 10, 128, 256], P(None, ('rec', 'gx')), parts along dimension 1, as said below
- omega: float32 [4, 256], replicated, may hold values from -6 to 6
Outputs:
- basis: bfloat16 [3, 96, 10, 128, 256], P(None, ('rec', 'gx')), parts along dimension 1
- factor: float32 [512, 256], P('rec'), parts along dimension 0
There are 2 independent parts, one for each index of `rec`. A program takes and returns all parts, laid end to end along the dimension named above; an argument that names none is the same for every part. Nothing has to cross between parts.
Inputs may be any that keep to these rules, and one draw needn't show every extreme that they name: `sketch_old`: finite values of order one; rows differ in scale. `velocity`: finite values. `span_rim`: finite values.
All inputs are finite; a program needn't handle non-finite values.
Results may differ from a plain program's by a relative error of at most 0.014.
The roundings to bfloat16 on the way count: a program that leaves them out, or rounds other values in their place, can miss the bound.
Values sent between devices are 32-bit elements; how exact they have to be, the bound alone decides.
No kernel may reach another device: no remote copies, remote signals or barrier semaphores. Data moves between devices by JAX's collectives and lax.ppermute only.
A program may use at most 64 MiB of HBM per device.

v0:
```python
import jax
import jax.numpy as jnp
from jax import lax
from jax.sharding import PartitionSpec as P

COEFS = (0.75, -0.15, 1.0 / 60.0)


def extended_2(cells, sides, width):
    for axis, dim in sides:
        count = lax.axis_size(axis)
        head = lax.slice_in_dim(cells, 0, width, axis=dim)
        tail = lax.slice_in_dim(cells, cells.shape[dim] - width, cells.shape[dim], axis=dim)
        cells = jnp.concatenate(
            [
                lax.ppermute(tail, axis, [(i, (i + 1) % count) for i in range(count)]),
                cells,
                lax.ppermute(head, axis, [((i + 1) % count, i) for i in range(count)]),
            ],
            axis=dim,
        )
    return cells


def band_diff(padded, axis, count):
    out_shape = list(padded.shape)
    out_shape[axis] = count
    total = jnp.zeros(tuple(out_shape), jnp.float32)
    for shift_k, weight in zip((1, 2, 3), COEFS):
        ahead = lax.slice_in_dim(padded, 3 + shift_k, 3 + shift_k + count, axis=axis)
        behind = lax.slice_in_dim(padded, 3 - shift_k, 3 - shift_k + count, axis=axis)
        total = total + weight * (ahead - behind)
    return total


def span_extend(field, rim_part):
    return jnp.concatenate([rim_part[..., :3], field, rim_part[..., 3:]], axis=-1)


def upper_factor(gram):
    order = gram.shape[0]
    index = jnp.arange(order, dtype=jnp.int32)

    def column_step(j, lower):
        pick = (index == j).astype(gram.dtype)
        row = jnp.dot(pick, lower, precision=lax.Precision.HIGHEST)
        column = jnp.dot(gram, pick, precision=lax.Precision.HIGHEST) - jnp.dot(
            lower, row, precision=lax.Precision.HIGHEST
        )
        pivot = jnp.sqrt(jnp.sum(column * pick))
        below = (index > j).astype(gram.dtype)
        fresh = column * below / pivot + pick * pivot
        return lower + fresh[:, None] * pick[None, :]

    lower = lax.fori_loop(0, order, column_step, jnp.zeros_like(gram))
    return lower.T


def inverse_upper(upper):
    order = upper.shape[0]
    index = jnp.arange(order, dtype=jnp.int32)
    lower = upper.T

    def row_step(j, solved):
        pick = (index == j).astype(upper.dtype)
        row = jnp.dot(pick, lower, precision=lax.Precision.HIGHEST)
        pivot = jnp.sum(row * pick)
        fresh = (pick - jnp.dot(row, solved, precision=lax.Precision.HIGHEST)) / pivot
        return solved + pick[:, None] * fresh[None, :]

    solved = lax.fori_loop(0, order, row_step, jnp.zeros_like(upper))
    return solved.T


def gram_of(matrix):
    return lax.dot_general(
        matrix, matrix, (((0,), (0,)), ((), ())), preferred_element_type=jnp.float32
    )


def local(velocity, span_rim, sketch_old, omega):
    slabs = velocity.shape[2]
    band_rows = velocity.shape[3] - 6
    span_cells = velocity.shape[4]
    extended = extended_2(velocity, (("gx", 2),), 3)
    v_ext = extended[:, 1, :, 3 : 3 + band_rows]
    w_ext = extended[:, 2, :, 3 : 3 + band_rows]
    band = velocity[:, :, :, 3 : 3 + band_rows]
    u_span = span_extend(band[:, 0], span_rim[:, 0])
    v_span = span_extend(band[:, 1], span_rim[:, 1])
    vort_x = band_diff(velocity[:, 2], 2, band_rows) - band_diff(v_span, 3, span_cells)
    vort_y = band_diff(u_span, 3, span_cells) - band_diff(w_ext, 1, slabs)
    vort_z = band_diff(v_ext, 1, slabs) - band_diff(velocity[:, 0], 2, band_rows)
    vort = jnp.stack([vort_x, vort_y, vort_z], axis=1)
    sketch = sketch_old.astype(jnp.float32)
    for snap in range(vort.shape[0]):
        sketch = sketch + vort[snap][..., None] * omega[snap]
    sketch = sketch.astype(jnp.bfloat16)
    matrix = sketch.reshape(-1, sketch.shape[-1])
    total = jnp.float32(matrix.shape[0] * lax.axis_size("gx"))
    local_gram = gram_of(matrix) / total
    gram = lax.psum(local_gram, "gx")
    lower = lax.linalg.cholesky(gram, symmetrize_input=False)
    factor = lower.T
    eye = jnp.eye(gram.shape[0], dtype=gram.dtype)
    lower_inv = lax.linalg.triangular_solve(lower, eye, left_side=True, lower=True)
    inverse_one = lower_inv.T.astype(jnp.bfloat16)
    basis = jnp.dot(matrix, inverse_one, preferred_element_type=jnp.float32).astype(jnp.bfloat16)
    return (basis.reshape(sketch.shape), factor)


def solution(mesh):
    in_specs = (
        P(None, None, ("rec", "gx"), None, None),
        P(None, None, ("rec", "gx"), None, None),
        P(None, ("rec", "gx"), None, None, None),
        P(),
    )
    out_specs = (P(None, ("rec", "gx"), None, None, None), P("rec", None))
    return jax.shard_map(local, mesh=mesh, in_specs=in_specs, out_specs=out_specs, check_vma=False)
```

profile of v0, /device:TPU:1, one launch (start us, length us, event | category | flops | bytes accessed | tf_op | source)
XLA Modules:
  0.0 201.3 jit_solution(16693057301777906816)
XLA Ops:
  7.3 2.6 %collective-permute-start = (f32[4,3,3,16,128]{4,3,2,1,0:T(8,128)}, f32[4,3,3,16,128]{4,3,2,1,0:T(8,128)S(1)}, u32[]{:S(2)}, u32[]{:S(2)}) collective-permute-start(f32[4,3,3,16,128]{4,3,2,1,0:T(8,128)} %param.4), channel_id=1, source_target_pairs={{0,1},{1,2},{2,3},{3,4},{4,5},{5,6},{6,7},{7,8},{8,9},{9,10},{10,1... | collective-permute-start | bytes 884744 | tf_op jit(solution)/shard_map/ppermute | solution.py:16
  9.9 1.0 slice_bitcast_fusion.5
  10.9 1.0 slice_bitcast_fusion.4
  11.9 1.0 fusion.64
  13.3 0.4 fusion.26
  13.6 0.8 fusion.67
  14.8 2.3 %collective-permute-done = f32[4,3,3,16,128]{4,3,2,1,0:T(8,128)S(1)} collective-permute-done((f32[4,3,3,16,128]{4,3,2,1,0:T(8,128)}, f32[4,3,3,16,128]{4,3,2,1,0:T(8,128)S(1)}, u32[]{:S(2)}, u32[]{:S(2)}) %collective-permute-start) | collective-permute-done | bytes 294944 | tf_op jit(solution)/shard_map/ppermute | solution.py:16
  17.1 1.0 constant_dynamic-update-slice_fusion.1
  18.3 0.3 fusion.14
  18.7 7.5 %add_convert_fusion = bf16[3,3,10,128,256]{4,3,2,1,0:T(8,128)(2,1)S(1)} fusion(bf16[3,3,10,128,256]{4,3,2,1,0:T(8,128)(2,1)S(1)} %copy-done.1, f32[256]{0:T(256)S(1)} %bitcast.90, f32[3,3,10,128]{3,2,1,0:T(8,128)S(1)} %get-tuple-element.27, f32[256]{0:T(256)S(1)} %bitcast.91, f32[3,3,10,128]{3,2,1,0:T(8,128)S(1)} %get-tuple-element.28, f32[256]{0:T(256)S(1)} %bitcast.89, ...), kind=kLoop, calls=%fused_computation.3 | loop fusion | flops 29491200 | bytes 11984896 | tf_op jit(solution)/shard_map/convert_element_type | solution.py:98
  26.3 2.5 %copy-done = bf16[3,3,10,128,256]{4,3,2,1,0:T(8,128)(2,1)} copy-done((bf16[3,3,10,128,256]{4,3,2,1,0:T(8,128)(2,1)}, bf16[3,3,10,128,256]{4,3,2,1,0:T(8,128)(2,1)S(1)}, u32[]{:S(2)}) %copy-start) | copy-done | bytes 5898264
  28.8 2.4 %fusion = f32[256,256]{1,0:T(8,128)} fusion(bf16[3,3,10,128,256]{4,3,2,1,0:T(8,128)(2,1)S(1)} %add_convert_fusion), kind=kOutput, calls=%fused_computation.5 | convolution fusion | flops 1510014976 | bytes 6160384 | tf_op jit(solution)/shard_map/dot_general | solution.py:76
  31.3 91.7 %all-reduce.3.cloned.1.call-done = f32[256,256]{1,0:T(8,128)} async-done(((f32[256,256]{1,0:T(8,128)}), f32[256,256]{1,0:T(8,128)}) %all-reduce.3.cloned.1.call-update) | async-done | bytes 262160 | tf_op jit(solution)/shard_map/psum | solution.py:102
  123.0 0.8 cholesky.118
  123.8 11.7 %cholesky.50 = f32[128,128]{1,0:T(8,128)S(1)} custom-call(f32[128,128]{1,0:T(8,128)S(1)} %cholesky.118), custom_call_target="Cholesky" | custom-call | tf_op jit(solution)/shard_map/cholesky | solution.py:103
  135.6 0.6 compare_reduce_fusion.1
  136.2 9.8 %custom-call.11 = f32[1,128,128]{1,2,0:T(8,128)S(1)} custom-call(f32[1,128,128]{2,1,0:T(8,128)S(1)} %get-tuple-element.41), custom_call_target="InvertDiagBlocksLowerTriangular" | custom-call | tf_op jit(solution)/shard_map/cholesky | solution.py:103
  146.1 1.0 constant_dynamic-update-slice_fusion.4
  147.1 1.1 convolution_subtract_fusion.1
  148.2 11.7 %cholesky.105 = f32[128,128]{1,0:T(8,128)S(1)} custom-call(f32[128,128]{1,0:T(8,128)S(1)} %convolution_subtract_fusion.1), custom_call_target="Cholesky" | custom-call | tf_op jit(solution)/shard_map/cholesky | solution.py:103
  160.0 0.7 compare_reduce_fusion
  162.0 1.0 copy.29
  163.0 3.8 %while.1 = (s32[]{:T(128)}, f32[256,256]{1,0:T(8,128)S(1)}, s32[2,2]{1,0:T(2,128)S(1)}, f32[2,128,128]{2,1,0:T(8,128)S(1)}, s32[]{:T(128)}) while((s32[]{:T(128)}, f32[256,256]{1,0:T(8,128)S(1)}, s32[2,2]{1,0:T(2,128)S(1)}, f32[2,128,128]{2,1,0:T(8,128)S(1)}, s32[]{:T(128)}) %tuple.43), condition=%wide.while_cond, body=%wide.while_body.sunk | while | flops 2 | bytes 131189 | solution.py:106
  163.0 0.6 fusion.77
  163.7 1.3 bitcast_dynamic-update-slice_fusion.2
  165.0 0.6 fusion.77
  165.6 1.3 bitcast_dynamic-update-slice_fusion.2
  166.9 19.7 %custom-call.12 = f32[2,128,128]{1,2,0:T(8,128)S(1)} custom-call(f32[2,128,128]{2,1,0:T(8,128)S(1)} %get-tuple-element.9), custom_call_target="InvertDiagBlocksLowerTriangular" | custom-call | tf_op jit(solution)/shard_map/triangular_solve | solution.py:106
  186.6 0.3 fusion.68
  186.8 0.3 convolution_subtract_fusion
  187.1 0.3 convolution_convert_fusion.1
  187.4 7.0 %convolution_convert_fusion = bf16[11520,256]{1,0:T(8,128)(2,1)} fusion(bf16[11520,256]{1,0:T(8,128)(2,1)} %bitcast.86, bf16[128,256]{1,0:T(8,128)(2,1)S(1)} %convolution_convert_fusion.1, bf16[128,256]{1,0:T(8,128)(2,1)S(1)} %get-tuple-element.52), kind=kOutput, calls=%fused_computation.2 | convolution fusion | flops 1513160704 | bytes 11927552 | tf_op jit(solution)/shard_map/dot_general | solution.py:108
  (30 shorter events, 1.3 us)
Async XLA Ops:
  7.2 115.8 %all-reduce.3.cloned.1.call-start = ((), (), s32[]{:S(2)}) async-start(), calls=%async_computation | async-start | bytes 524288 | tf_op jit(solution)/shard_map/psum | solution.py:102
  7.2 10.9 %collective-permute-start.1 = (f32[4,3,3,16,128]{4,3,2,1,0:T(8,128)}, f32[4,3,3,16,128]{4,3,2,1,0:T(8,128)S(1)}, u32[]{:S(2)}, u32[]{:S(2)}) collective-permute-start(f32[4,3,3,16,128]{4,3,2,1,0:T(8,128)} %param.4), channel_id=1, source_target_pairs={{1,0},{2,1},{3,2},{4,3},{5,4},{6,5},{7,6},{8,7},{9,8},{10,9},{11,1... | collective-permute-start | bytes 884744 | tf_op jit(solution)/shard_map/ppermute | solution.py:18
  7.3 9.8 %collective-permute-start = (f32[4,3,3,16,128]{4,3,2,1,0:T(8,128)}, f32[4,3,3,16,128]{4,3,2,1,0:T(8,128)S(1)}, u32[]{:S(2)}, u32[]{:S(2)}) collective-permute-start(f32[4,3,3,16,128]{4,3,2,1,0:T(8,128)} %param.4), channel_id=1, source_target_pairs={{0,1},{1,2},{2,3},{3,4},{4,5},{5,6},{6,7},{7,8},{8,9},{9,10},{10,1... | collective-permute-start | bytes 884744 | tf_op jit(solution)/shard_map/ppermute | solution.py:16
  14.8 3.9 %copy-start.1 = (bf16[3,3,10,128,256]{4,3,2,1,0:T(8,128)(2,1)S(1)}, bf16[3,3,10,128,256]{4,3,2,1,0:T(8,128)(2,1)}, u32[]{:S(2)}) copy-start(bf16[3,3,10,128,256]{4,3,2,1,0:T(8,128)(2,1)} %param.6) | copy-start | bytes 17694724
  26.3 2.5 %copy-start = (bf16[3,3,10,128,256]{4,3,2,1,0:T(8,128)(2,1)}, bf16[3,3,10,128,256]{4,3,2,1,0:T(8,128)(2,1)S(1)}, u32[]{:S(2)}) copy-start(bf16[3,3,10,128,256]{4,3,2,1,0:T(8,128)(2,1)S(1)} %add_convert_fusion) | copy-start | bytes 17694724
Sparse Core Ops, SparseCore 0:
  31.4 91.5 all-reduce.2
where the time goes:
time: 202 us; the launch traced here: 201 us
  waiting for transfers between devices  94 us (47%)
  other arithmetic  62.7 us (31%)
  between operations  15.5 us (8%)
  local copies, waits for them, and re-layouts  13.9 us (7%)
  matrix products  12.4 us (6%)
  starting transfers between devices  2.76 us (1%)
    psum x1, waiting for transfers between devices, local(): gram = lax.psum(local_gram, 'gx')  91.7 us
    another operation x7, other arithmetic, local(): lower = lax.linalg.cholesky(gram, symmetrize_input=False)  34.6 us
    another operation x2, other arithmetic, local(): lax.linalg.triangular_solve(lower, eye, left_side=True, lower=True)  19.7 us
    convert_element_type x1, other arithmetic, local(): sketch = sketch.astype(jnp.bfloat16)  7.55 us
    dot_general x1, matrix products, local(): jnp.dot(matrix, inverse_one, preferred_element_type=jnp.float32)  6.98 us
    unnamed x7, local copies, waits for them, and re-layouts  4.54 us
  transfers between devices with their start and end apart: 3, of which 2 were waited for; matrix products, arithmetic and copies ran while one was open for 3% of the time, Pallas kernels for 0%

commit v1 on v0

--- a/solution.py
+++ b/solution.py
@@ -99,7 +99,7 @@
     matrix = sketch.reshape(-1, sketch.shape[-1])
     total = jnp.float32(matrix.shape[0] * lax.axis_size("gx"))
     local_gram = gram_of(matrix) / total
-    gram = lax.psum(local_gram, "gx")
+    gram = jnp.sum(lax.all_gather(local_gram, "gx"), axis=0)
     lower = lax.linalg.cholesky(gram, symmetrize_input=False)
     factor = lower.T
     eye = jnp.eye(gram.shape[0], dtype=gram.dtype)

time: 202 us -> 163 us (0.81)
  waiting for transfers between devices: 94 us -> 55.5 us
  other arithmetic: 62.7 us -> 65.3 us
    psum x1 -> x0, waiting for transfers between devices: 91.7 us -> none  [local(): gram = lax.psum(local_gram, 'gx')]
    all_gather x0 -> x1, waiting for transfers between devices: none -> 53.2 us  [local(): gram = jnp.sum(lax.all_gather(local_gram, 'gx'), axis=0)]
    reduce_sum x0 -> x1, other arithmetic: none -> 2.48 us  [local(): gram = jnp.sum(lax.all_gather(local_gram, 'gx'), axis=0)]
  transfers between devices with their start and end apart: 3 -> 3, of which waited for: 2 -> 2; matrix products, arithmetic and copies ran while one was open for 3% -> 4% of each run, Pallas kernels for 0% -> 0%
where the time goes in v1:
time: 163 us
  other arithmetic  65.3 us (40%)
  waiting for transfers between devices  55.5 us (34%)
  between operations  15.5 us (10%)
  local copies, waits for them, and re-layouts  12.9 us (8%)
  matrix products  10.7 us (7%)
  starting transfers between devices  2.76 us (2%)
    all_gather x1, waiting for transfers between devices, local(): gram = jnp.sum(lax.all_gather(local_gram, 'gx'), axis=0)  53.2 us
    another operation x7, other arithmetic, local(): lower = lax.linalg.cholesky(gram, symmetrize_input=False)  34.7 us
    another operation x2, other arithmetic, local(): lax.linalg.triangular_solve(lower, eye, left_side=True, lower=True)  19.7 us
    convert_element_type x1, other arithmetic, local(): sketch = sketch.astype(jnp.bfloat16)  7.55 us
    dot_general x1, matrix products, local(): jnp.dot(matrix, inverse_one, preferred_element_type=jnp.float32)  6.98 us
    unnamed x7, local copies, waits for them, and re-layouts  4.36 us
    another operation x6, local copies, waits for them, and re-layouts  3.81 us
  transfers between devices with their start and end apart: 3, of which 2 were waited for; matrix products, arithmetic and copies ran while one was open for 4% of the time, Pallas kernels for 0%

profile of v1, /device:TPU:1, one launch (start us, length us, event | category | flops | bytes accessed | tf_op | source)
XLA Modules:
  0.0 162.7 jit_solution(17976625191389136886)
XLA Ops:
  7.3 2.6 %collective-permute-start = (f32[4,3,3,16,128]{4,3,2,1,0:T(8,128)}, f32[4,3,3,16,128]{4,3,2,1,0:T(8,128)S(1)}, u32[]{:S(2)}, u32[]{:S(2)}) collective-permute-start(f32[4,3,3,16,128]{4,3,2,1,0:T(8,128)} %param.4), channel_id=1, source_target_pairs={{0,1},{1,2},{2,3},{3,4},{4,5},{5,6},{6,7},{7,8},{8,9},{9,10},{10,1... | collective-permute-start | bytes 884744 | tf_op jit(solution)/shard_map/ppermute | solution.py:16
  9.9 1.0 slice_bitcast_fusion.5
  10.9 1.0 slice_bitcast_fusion.4
  11.9 1.0 fusion.64
  13.3 0.4 fusion.26
  13.6 0.8 fusion.67
  14.8 2.3 %collective-permute-done = f32[4,3,3,16,128]{4,3,2,1,0:T(8,128)S(1)} collective-permute-done((f32[4,3,3,16,128]{4,3,2,1,0:T(8,128)}, f32[4,3,3,16,128]{4,3,2,1,0:T(8,128)S(1)}, u32[]{:S(2)}, u32[]{:S(2)}) %collective-permute-start) | collective-permute-done | bytes 294944 | tf_op jit(solution)/shard_map/ppermute | solution.py:16
  17.1 1.0 constant_dynamic-update-slice_fusion.1
  18.3 0.3 fusion.14
  18.7 7.5 %add_convert_fusion = bf16[3,3,10,128,256]{4,3,2,1,0:T(8,128)(2,1)S(1)} fusion(bf16[3,3,10,128,256]{4,3,2,1,0:T(8,128)(2,1)S(1)} %copy-done.1, f32[256]{0:T(256)S(1)} %bitcast.92, f32[3,3,10,128]{3,2,1,0:T(8,128)S(1)} %get-tuple-element.27, f32[256]{0:T(256)S(1)} %bitcast.93, f32[3,3,10,128]{3,2,1,0:T(8,128)S(1)} %get-tuple-element.28, f32[256]{0:T(256)S(1)} %bitcast.91, ...), kind=kLoop, calls=%fused_computation.3 | loop fusion | flops 29491200 | bytes 11984896 | tf_op jit(solution)/shard_map/convert_element_type | solution.py:98
  26.3 2.5 %copy-done = bf16[3,3,10,128,256]{4,3,2,1,0:T(8,128)(2,1)} copy-done((bf16[3,3,10,128,256]{4,3,2,1,0:T(8,128)(2,1)}, bf16[3,3,10,128,256]{4,3,2,1,0:T(8,128)(2,1)S(1)}, u32[]{:S(2)}) %copy-start) | copy-done | bytes 5898264
  28.8 2.4 %fusion = f32[256,256]{1,0:T(8,128)} fusion(bf16[3,3,10,128,256]{4,3,2,1,0:T(8,128)(2,1)S(1)} %add_convert_fusion), kind=kOutput, calls=%fused_computation.5 | convolution fusion | flops 1510014976 | bytes 6160384 | tf_op jit(solution)/shard_map/dot_general | solution.py:76
  31.3 53.2 %all-gather.3.cloned.1.call-done = f32[4096,256]{1,0:T(8,128)} async-done(((f32[256,256]{1,0:T(8,128)}), f32[4096,256]{1,0:T(8,128)}) %all-gather.3.cloned.1.call-update) | async-done | bytes 4194320 | tf_op jit(solution)/shard_map/all_gather | solution.py:102
  84.5 2.5 %reduce_sum.9 = f32[256,256]{1,0:T(8,128)S(1)} reduce(f32[16,256,256]{2,1,0:T(8,128)} %bitcast.89, f32[]{:T(128)} %constant.58.clone.1), dimensions={0}, to_apply=%region_0.0 | reduce | flops 983040 | bytes 4456452 | tf_op jit(solution)/shard_map/reduce_sum | solution.py:102
  87.0 11.7 %cholesky.50 = f32[128,128]{1,0:T(8,128)S(1)} custom-call(f32[128,128]{1,0:T(8,128)S(1)} %cholesky.118), custom_call_target="Cholesky" | custom-call | tf_op jit(solution)/shard_map/cholesky | solution.py:103
  98.8 0.6 compare_reduce_fusion.1
  99.4 9.8 %custom-call.11 = f32[1,128,128]{1,2,0:T(8,128)S(1)} custom-call(f32[1,128,128]{2,1,0:T(8,128)S(1)} %get-tuple-element.41), custom_call_target="InvertDiagBlocksLowerTriangular" | custom-call | tf_op jit(solution)/shard_map/cholesky | solution.py:103
  109.2 0.2 constant_dynamic-update-slice_fusion.4
  109.4 0.3 convolution_subtract_fusion.1
  109.7 11.8 %cholesky.105 = f32[128,128]{1,0:T(8,128)S(1)} custom-call(f32[128,128]{1,0:T(8,128)S(1)} %convolution_subtract_fusion.1), custom_call_target="Cholesky" | custom-call | tf_op jit(solution)/shard_map/cholesky | solution.py:103
  121.5 0.7 compare_reduce_fusion
  123.5 0.8 copy.29
  124.4 3.8 %while.1 = (s32[]{:T(128)}, f32[256,256]{1,0:T(8,128)S(1)}, s32[2,2]{1,0:T(2,128)S(1)}, f32[2,128,128]{2,1,0:T(8,128)S(1)}, s32[]{:T(128)}) while((s32[]{:T(128)}, f32[256,256]{1,0:T(8,128)S(1)}, s32[2,2]{1,0:T(2,128)S(1)}, f32[2,128,128]{2,1,0:T(8,128)S(1)}, s32[]{:T(128)}) %tuple.43), condition=%wide.while_cond, body=%wide.while_body.sunk | while | flops 2 | bytes 131189 | solution.py:106
  124.4 0.6 fusion.77
  125.1 1.3 bitcast_dynamic-update-slice_fusion.2
  126.4 0.6 fusion.77
  127.0 1.3 bitcast_dynamic-update-slice_fusion.2
  128.3 19.7 %custom-call.12 = f32[2,128,128]{1,2,0:T(8,128)S(1)} custom-call(f32[2,128,128]{2,1,0:T(8,128)S(1)} %get-tuple-element.9), custom_call_target="InvertDiagBlocksLowerTriangular" | custom-call | tf_op jit(solution)/shard_map/triangular_solve | solution.py:106
  148.0 0.3 fusion.68
  148.2 0.3 convolution_subtract_fusion
  148.5 0.3 convolution_convert_fusion.1
  148.8 7.0 %convolution_convert_fusion = bf16[11520,256]{1,0:T(8,128)(2,1)} fusion(bf16[11520,256]{1,0:T(8,128)(2,1)} %bitcast.87, bf16[128,256]{1,0:T(8,128)(2,1)S(1)} %convolution_convert_fusion.1, bf16[128,256]{1,0:T(8,128)(2,1)S(1)} %get-tuple-element.52), kind=kOutput, calls=%fused_computation.2 | convolution fusion | flops 1513160704 | bytes 11927552 | tf_op jit(solution)/shard_map/dot_general | solution.py:108
  (31 shorter events, 1.3 us)
Async XLA Ops:
  7.2 77.3 %all-gather.3.cloned.1.call-start = ((), (), s32[]{:S(2)}) async-start(), calls=%async_computation | async-start | bytes 4456448 | tf_op jit(solution)/shard_map/all_gather | solution.py:102
  7.2 10.9 %collective-permute-start.1 = (f32[4,3,3,16,128]{4,3,2,1,0:T(8,128)}, f32[4,3,3,16,128]{4,3,2,1,0:T(8,128)S(1)}, u32[]{:S(2)}, u32[]{:S(2)}) collective-permute-start(f32[4,3,3,16,128]{4,3,2,1,0:T(8,128)} %param.4), channel_id=1, source_target_pairs={{1,0},{2,1},{3,2},{4,3},{5,4},{6,5},{7,6},{8,7},{9,8},{10,9},{11,1... | collective-permute-start | bytes 884744 | tf_op jit(solution)/shard_map/ppermute | solution.py:18
  7.3 9.8 %collective-permute-start = (f32[4,3,3,16,128]{4,3,2,1,0:T(8,128)}, f32[4,3,3,16,128]{4,3,2,1,0:T(8,128)S(1)}, u32[]{:S(2)}, u32[]{:S(2)}) collective-permute-start(f32[4,3,3,16,128]{4,3,2,1,0:T(8,128)} %param.4), channel_id=1, source_target_pairs={{0,1},{1,2},{2,3},{3,4},{4,5},{5,6},{6,7},{7,8},{8,9},{9,10},{10,1... | collective-permute-start | bytes 884744 | tf_op jit(solution)/shard_map/ppermute | solution.py:16
  14.8 3.9 %copy-start.1 = (bf16[3,3,10,128,256]{4,3,2,1,0:T(8,128)(2,1)S(1)}, bf16[3,3,10,128,256]{4,3,2,1,0:T(8,128)(2,1)}, u32[]{:S(2)}) copy-start(bf16[3,3,10,128,256]{4,3,2,1,0:T(8,128)(2,1)} %param.6) | copy-start | bytes 17694724
  26.3 2.5 %copy-start = (bf16[3,3,10,128,256]{4,3,2,1,0:T(8,128)(2,1)}, bf16[3,3,10,128,256]{4,3,2,1,0:T(8,128)(2,1)S(1)}, u32[]{:S(2)}) copy-start(bf16[3,3,10,128,256]{4,3,2,1,0:T(8,128)(2,1)S(1)} %add_convert_fusion) | copy-start | bytes 17694724
Sparse Core Ops, SparseCore 0:
  31.4 53.0 all-gather.2
